TPU v7x, 256 devices: a whole 4x4x8 slice. The times are simulated.
256 devices in a mesh: req: 32 (over y, z), vocab: 8 (over x, core).
Axes of the slice: x: 4, y: 4, z: 8, core: 2. Of those that a mesh axis runs over, the one named last changes fastest.
Arguments:
- draft_states: bfloat16 [64, 64, 1536], P('req')
- parents: int32 [64, 64], P('req'), may hold values from -1 to 62, as said below
- live_draft_count: int32 [64], replicated, may hold values from 32 to 64, as said below
- path_index: int32 [64, 8], P('req'), may hold values from 0 to 63, as said below
- cached_length_list: int32 [64], P('req'), may hold values from 256 to 1792, as said below
- cached_key_rows: bfloat16 [65536, 768], P('req', 'vocab')
- cached_value_rows: bfloat16 [65536, 768], P('req', 'vocab'), may hold values from -6 to 6
- attend_gain: bfloat16 [1536], replicated, may hold values from 0.099609375 to 1.8984375
- hidden_gain: bfloat16 [1536], replicated, may hold values from 0.099609375 to 1.8984375
- final_gain: bfloat16 [1536], replicated, may hold values from 0.099609375 to 1.8984375
- query_weight: bfloat16 [1536, 1536], P(None, 'vocab')
- key_matrix: bfloat16 [1536, 768], P(None, 'vocab')
- value_matrix: bfloat16 [1536, 768], P(None, 'vocab'), may hold values from -0.15625 to 0.15625
- out_weight: bfloat16 [1536, 1536], P('vocab'), may hold values from -0.15625 to 0.15625
- gate_weight: bfloat16 [1536, 4096], P(None, 'vocab'), may hold values from -0.15625 to 0.15625
- up_weight: bfloat16 [1536, 4096], P(None, 'vocab'), may hold values from -0.15625 to 0.15625
- down_weight: bfloat16 [4096, 1536], P('vocab'), may hold values from -0.09375 to 0.09375
- head_weight: bfloat16 [1536, 32000], P(None, 'req'), may hold values from -0.4375 to 0.4375
Outputs:
- layer_output_rows: bfloat16 [64, 64, 1536], P('req', None, 'vocab')
- accepted_keys: bfloat16 [64, 8, 768], P('req', None, 'vocab')
- accepted_values: bfloat16 [64, 8, 768], P('req', None, 'vocab')
- norm_values: float32 [64, 8], P('req', 'vocab')
- maxima: float32 [64, 8], P(None, 'vocab')
Inputs may be any that keep to these rules, and one draw needn't show every extreme that they name: `live_draft_count`: the counts of all requests sum to exactly 3072. `parents`: each draft token's parent lies below its own index; the first token's is -1. `path_index`: each row lists 8 live draft tokens of its request, each the parent of the next. `cached_length_list`: the lengths of the 2 requests of one index of req sum to at most 2048, and to exactly 2048 on a quarter of the indices of req (at least one); on such an index one request is long and the others hold 256 each.
All inputs are finite; a program needn't handle non-finite values.
Results may differ from a plain program's by a relative error of at most 0.012.
Values may be sent and summed in bfloat16 or wider, within the bound.
No kernel may reach another device: no remote copies, remote signals or barrier semaphores. Data moves between devices by JAX's collectives and lax.ppermute only.
A program may use at most 64 MiB of HBM per device.

v0:
```python
import jax
import jax.numpy as jnp
from jax import lax
from jax.sharding import PartitionSpec as P

HEAD_SIZE = 96
eps_norm = 1e-05
rope_base = 100000.0
masked_score = -1e30


def apply_rotation(values, token_positions):
    half_dim = values.shape[-1] // 2
    inverse = rope_base ** (-jnp.arange(half_dim, dtype=jnp.float32) * 2.0 / values.shape[-1])
    angles = token_positions.astype(jnp.float32)[:, None] * inverse[None, :]
    cosine = jnp.cos(angles)[:, None, :]
    sine_of = jnp.sin(angles)[:, None, :]
    first_half = values[..., :half_dim]
    second_half = values[..., half_dim:]
    return jnp.concatenate(
        [first_half * cosine - second_half * sine_of, second_half * cosine + first_half * sine_of],
        axis=-1,
    )


def ancestors(parents):
    draft_length = parents.shape[-1]
    columns = jnp.arange(draft_length, dtype=jnp.int32)
    reached = jnp.eye(draft_length, dtype=jnp.float32) + (parents[..., :, None] == columns).astype(
        jnp.float32
    )
    for sweep_number in range((draft_length - 1).bit_length()):
        reached = jnp.minimum(
            jnp.einsum("bij,bjk->bik", reached, reached, precision=lax.Precision.HIGHEST), 1.0
        )
    return reached


def lookup(entries, indices):
    matches = indices[:, None] == jnp.arange(entries.shape[0], dtype=jnp.int32)[None, :]
    return jnp.sum(jnp.where(matches, entries[None, :], 0), axis=1)


def span_scores(query_block, first, last, number, joined_keys, block_len):
    pool_rows = joined_keys.shape[0]
    nominal = first + number * block_len
    actual = jnp.minimum(nominal, pool_rows - block_len)
    keys_block = lax.dynamic_slice_in_dim(joined_keys, actual, block_len, 0)
    scores = jnp.einsum(
        "kqd,pkd->kqp", query_block, keys_block, preferred_element_type=jnp.float32
    ) * query_block.shape[-1] ** (-0.5)
    slots = actual + jnp.arange(block_len, dtype=jnp.int32)
    allowed = (slots >= nominal) & (slots < jnp.minimum(last, nominal + block_len))
    return (scores, allowed[None, None, :], actual)


def span_max(query_block, first, last, joined_keys, block_len):
    block_count = (last - first + block_len - 1) // block_len

    def step(number, running):
        scores, allowed, actual = span_scores(
            query_block, first, last, number, joined_keys, block_len
        )
        return jnp.maximum(running, jnp.max(jnp.where(allowed, scores, masked_score), axis=2))

    start_max = jnp.full(query_block.shape[:2], masked_score, jnp.float32)
    return lax.fori_loop(0, block_count, step, start_max)


def span_sums(query_block, first, last, top, joined_keys, joined_values, block_len):
    block_count = (last - first + block_len - 1) // block_len

    def step(number, running):
        totals_now, weighted_now = running
        scores, allowed, actual = span_scores(
            query_block, first, last, number, joined_keys, block_len
        )
        weights = jnp.where(allowed, jnp.exp(scores - top[:, :, None]), 0.0).astype(jnp.bfloat16)
        values_block = lax.dynamic_slice_in_dim(joined_values, actual, block_len, 0)
        return (
            totals_now + jnp.sum(weights.astype(jnp.float32), axis=2),
            weighted_now
            + jnp.einsum("kqp,pkd->kqd", weights, values_block, preferred_element_type=jnp.float32),
        )

    start_sums = (
        jnp.zeros(query_block.shape[:2], jnp.float32),
        jnp.zeros(query_block.shape, jnp.float32),
    )
    return lax.fori_loop(0, block_count, step, start_sums)


def maxima_over(query_sets, firsts, lasts, joined_keys, block_len):
    return lax.map(
        lambda item: span_max(item[0], item[1], item[2], joined_keys, block_len),
        (query_sets, firsts, lasts),
    )


def sums_over(query_sets, firsts, lasts, tops, joined_keys, joined_values, block_len):
    return lax.map(
        lambda item: span_sums(
            item[0], item[1], item[2], item[3], joined_keys, joined_values, block_len
        ),
        (query_sets, firsts, lasts, tops),
    )


def feed_forward(hidden_in, gate_weight, up_weight, down_weight):
    gate_out = jnp.dot(hidden_in, gate_weight, preferred_element_type=jnp.float32)
    up_out = jnp.dot(hidden_in, up_weight, preferred_element_type=jnp.float32)
    hidden = (jax.nn.silu(gate_out) * up_out).astype(jnp.bfloat16)
    partial_sum = jnp.dot(hidden, down_weight, preferred_element_type=jnp.float32)
    summed = lax.psum(partial_sum.astype(jnp.bfloat16), "vocab")
    return summed


def per_device(
    draft_states,
    parents,
    live_draft_count,
    path_index,
    cached_length_list,
    cached_key_rows,
    cached_value_rows,
    attend_gain,
    hidden_gain,
    final_gain,
    query_weight,
    key_matrix,
    value_matrix,
    out_weight,
    gate_weight,
    up_weight,
    down_weight,
    head_weight,
):
    local_requests, draft_length, model_width = draft_states.shape
    token_rows = local_requests * draft_length
    request_shards = lax.axis_size("req")
    request_shard = lax.axis_index("req")
    vocab_shards = lax.axis_size("vocab")
    vocab_shard = lax.axis_index("vocab")
    head_dim = HEAD_SIZE
    key_local = key_matrix.shape[1] // head_dim
    query_local = query_weight.shape[1] // head_dim
    group_factor = query_local // key_local
    pool_rows = cached_key_rows.shape[0]
    rows_per_request = draft_length * group_factor
    states = draft_states.reshape(token_rows, model_width).astype(jnp.float32)
    normalized_states = (
        states
        * lax.rsqrt(jnp.mean(states * states, axis=1, keepdims=True) + eps_norm)
        * attend_gain.astype(jnp.float32)
    ).astype(jnp.bfloat16)
    reached = ancestors(parents)
    token_positions = (
        cached_length_list[:, None] + (jnp.sum(reached, axis=2) - 1.0).astype(jnp.int32)
    ).reshape(token_rows)
    query_vectors = apply_rotation(
        jnp.dot(normalized_states, query_weight, preferred_element_type=jnp.float32).reshape(
            token_rows, query_local, head_dim
        ),
        token_positions,
    ).astype(jnp.bfloat16)
    fresh_keys = apply_rotation(
        jnp.dot(normalized_states, key_matrix, preferred_element_type=jnp.float32).reshape(
            token_rows, key_local, head_dim
        ),
        token_positions,
    ).astype(jnp.bfloat16)
    fresh_values = (
        jnp.dot(normalized_states, value_matrix, preferred_element_type=jnp.float32)
        .astype(jnp.bfloat16)
        .reshape(token_rows, key_local, head_dim)
    )
    query_rows = (
        query_vectors.reshape(token_rows, key_local, group_factor, head_dim)
        .transpose(1, 0, 2, 3)
        .reshape(key_local, token_rows * group_factor, head_dim)
    )
    score_scale = head_dim ** (-0.5)
    same_request = jnp.eye(local_requests, dtype=jnp.float32)
    tree_mask = (
        jnp.einsum("jk,jim->jikm", same_request, reached).reshape(token_rows, token_rows) > 0.5
    )
    tree_mask = jnp.repeat(tree_mask, group_factor, axis=0)[None]
    tree_scores = (
        jnp.einsum("kqd,rkd->kqr", query_rows, fresh_keys, preferred_element_type=jnp.float32)
        * score_scale
    )
    tree_max = jnp.max(jnp.where(tree_mask, tree_scores, masked_score), axis=2)
    tree_top = tree_max.reshape(key_local, local_requests, rows_per_request).transpose(1, 0, 2)
    cache_end = jnp.cumsum(cached_length_list)
    cache_start = cache_end - cached_length_list
    block_len = min(512, pool_rows)
    pool_keys = cached_key_rows.reshape(pool_rows, key_local, head_dim)
    pool_values = cached_value_rows.reshape(pool_rows, key_local, head_dim)
    by_request = query_rows.reshape(
        key_local, local_requests, rows_per_request, head_dim
    ).transpose(1, 0, 2, 3)
    pool_max = maxima_over(by_request, cache_start, cache_end, pool_keys, block_len)
    top = jnp.maximum(tree_top, pool_max)
    pool_totals, pool_weighted = sums_over(
        by_request, cache_start, cache_end, top, pool_keys, pool_values, block_len
    )
    top_rows = top.transpose(1, 0, 2).reshape(key_local, token_rows * group_factor)
    tree_weights = jnp.where(tree_mask, jnp.exp(tree_scores - top_rows[:, :, None]), 0.0).astype(
        jnp.bfloat16
    )
    totals = jnp.sum(tree_weights.astype(jnp.float32), axis=2) + pool_totals.transpose(
        1, 0, 2
    ).reshape(key_local, token_rows * group_factor)
    weighted_values = jnp.einsum(
        "kqr,rkd->kqd", tree_weights, fresh_values, preferred_element_type=jnp.float32
    )
    weighted_values = weighted_values + pool_weighted.transpose(1, 0, 2, 3).reshape(
        key_local, token_rows * group_factor, head_dim
    )
    attended = (
        (weighted_values / totals[:, :, None])
        .reshape(key_local, token_rows, group_factor, head_dim)
        .transpose(1, 0, 2, 3)
    )
    attended = attended.reshape(token_rows, query_local * head_dim).astype(jnp.bfloat16)
    attend_part = jnp.dot(attended, out_weight, preferred_element_type=jnp.float32)
    share_width = model_width // vocab_shards
    share_start = vocab_shard * share_width
    residual = states + lax.psum(attend_part, "vocab")
    hidden_in = (
        residual
        * lax.rsqrt(jnp.mean(residual * residual, axis=1, keepdims=True) + eps_norm)
        * hidden_gain.astype(jnp.float32)
    ).astype(jnp.bfloat16)
    local_counts = lax.dynamic_slice_in_dim(
        live_draft_count, request_shard * local_requests, local_requests
    )
    device_totals = jnp.sum(live_draft_count.reshape(request_shards, local_requests), axis=1)
    device_ends = jnp.cumsum(device_totals)
    device_starts = device_ends - device_totals
    own_start = lax.dynamic_index_in_dim(device_starts, request_shard, keepdims=False)
    own_total = jnp.sum(local_counts)
    local_ends = jnp.cumsum(local_counts)
    local_starts = local_ends - local_counts
    token_number = jnp.arange(token_rows, dtype=jnp.int32)
    token_request = token_number // draft_length
    token_place = token_number % draft_length
    live_rows = token_place < lookup(local_counts, token_request)
    slot_count = token_rows // request_shards
    even_rows = 3 * token_rows // 4
    slot_index = jnp.arange(request_shards * slot_count, dtype=jnp.int32)
    slot_target = slot_index // slot_count
    slot_order = slot_index % slot_count * request_shards
    send_rank = slot_order + (slot_target - own_start) % request_shards
    send_request = jnp.minimum(
        jnp.sum((local_ends[None, :] <= send_rank[:, None]).astype(jnp.int32), axis=1),
        local_requests - 1,
    )
    send_row = jnp.clip(
        send_request * draft_length + send_rank - lookup(local_starts, send_request),
        0,
        token_rows - 1,
    )
    outgoing = jnp.where(
        (send_rank < own_total)[:, None],
        jnp.take(hidden_in, send_row, axis=0),
        jnp.zeros((), jnp.bfloat16),
    )
    arrived = lax.all_to_all(outgoing, "req", split_axis=0, concat_axis=0, tiled=True)
    global_rank = jnp.arange(even_rows, dtype=jnp.int32) * request_shards + request_shard
    source = jnp.minimum(
        jnp.sum((device_ends[None, :] <= global_rank[:, None]).astype(jnp.int32), axis=1),
        request_shards - 1,
    )
    source_rank = global_rank - lookup(device_starts, source)
    packed = jnp.take(arrived, source * slot_count + source_rank // request_shards, axis=0)
    computed = feed_forward(packed, gate_weight, up_weight, down_weight)
    slot_starts = lookup(device_starts, slot_target)
    return_rank = slot_order + (request_shard - slot_starts) % request_shards
    return_live = return_rank < lookup(device_totals, slot_target)
    return_row = jnp.clip((slot_starts + return_rank) // request_shards, 0, even_rows - 1)
    backward = jnp.where(
        return_live[:, None], jnp.take(computed, return_row, axis=0), jnp.zeros((), jnp.bfloat16)
    )
    returned = lax.all_to_all(backward, "req", split_axis=0, concat_axis=0, tiled=True)
    local_rank = lookup(local_starts, token_request) + token_place
    home_slot = jnp.clip(
        (own_start + local_rank) % request_shards * slot_count + local_rank // request_shards,
        0,
        request_shards * slot_count - 1,
    )
    feed_rows = jnp.take(returned, home_slot, axis=0)
    updated = jnp.where(live_rows[:, None], residual + feed_rows.astype(jnp.float32), 0.0).astype(
        jnp.bfloat16
    )
    layer_part = lax.dynamic_slice_in_dim(updated, share_start, share_width, 1)
    path_length = path_index.shape[1]
    request_picker = (
        path_index[:, :, None] == jnp.arange(draft_length, dtype=jnp.int32)[None, None, :]
    ).astype(jnp.bfloat16)
    accepted_keys = jnp.einsum(
        "ytm,ymu->ytu",
        request_picker,
        fresh_keys.reshape(local_requests, draft_length, key_local * head_dim),
        preferred_element_type=jnp.float32,
    ).astype(jnp.bfloat16)
    accepted_values = jnp.einsum(
        "ytm,ymu->ytu",
        request_picker,
        fresh_values.reshape(local_requests, draft_length, key_local * head_dim),
        preferred_element_type=jnp.float32,
    ).astype(jnp.bfloat16)
    path_states = jnp.einsum(
        "ytm,ymu->ytu",
        request_picker,
        updated.reshape(local_requests, draft_length, updated.shape[1]),
        preferred_element_type=jnp.float32,
    ).astype(jnp.bfloat16)
    per_shard = path_length // vocab_shards
    head_rows = lax.dynamic_slice_in_dim(path_states, vocab_shard * per_shard, per_shard, 1)
    flat_rows = head_rows.reshape(local_requests * per_shard, model_width).astype(jnp.float32)
    mean_square = jnp.mean(flat_rows * flat_rows, axis=1)
    norm_values = jnp.sqrt(mean_square + eps_norm).reshape(local_requests, per_shard)
    head_in = (
        flat_rows * lax.rsqrt(mean_square + eps_norm)[:, None] * final_gain.astype(jnp.float32)
    ).astype(jnp.bfloat16)
    local_max = jnp.max(
        jnp.dot(
            lax.all_gather(head_in, "req", axis=0, tiled=True),
            head_weight,
            preferred_element_type=jnp.float32,
        ),
        axis=1,
    )
    maxima = lax.pmax(local_max, "req").reshape(request_shards * local_requests, per_shard)
    return (
        layer_part.reshape(local_requests, draft_length, share_width),
        accepted_keys,
        accepted_values,
        norm_values,
        maxima,
    )


def solution(mesh):
    in_specs = (
        P("req", None, None),
        P("req", None),
        P(),
        P("req", None),
        P("req"),
        P("req", "vocab"),
        P("req", "vocab"),
        P(),
        P(),
        P(),
        P(None, "vocab"),
        P(None, "vocab"),
        P(None, "vocab"),
        P("vocab", None),
        P(None, "vocab"),
        P(None, "vocab"),
        P("vocab", None),
        P(None, "req"),
    )
    out_specs = (
        P("req", None, "vocab"),
        P("req", None, "vocab"),
        P("req", None, "vocab"),
        P("req", "vocab"),
        P(None, "vocab"),
    )
    return jax.shard_map(
        per_device, mesh=mesh, in_specs=in_specs, out_specs=out_specs, check_vma=False
    )
```

profile of v0, /device:TPU:6, one launch (start us, length us, event | category | flops | bytes accessed | tf_op | source)
XLA Modules:
  0.0 430.9 jit_solution(2715974961499457239)
XLA Ops:
  7.8 1.4 reduce-window.24
  18.8 1.4 copy.72
  21.9 1.4 fusion.105
  25.5 1.6 maximum_bitcast_fusion
  27.1 14.0 %while.104 = (s32[]{:T(128)}, f32[2,1,128]{2,1,0:T(1,128)S(1)}, s32[2]{0:T(128)}, s32[2]{0:T(128)}, bf16[2,1,128,96]{3,2,1,0:T(8,128)(2,1)}, /*index=5*/bf16[204...) while((s32[]{:T(128)}, f32[2,1,128]{2,1,0:T(1,128)S(1)}, ...), condition=%wide.region_9.10_spmd, body=%wide.region_5.9_spmd.sunk | while | flops 12781597 | bytes 177346 | solution.py:94
  31.6 2.5 while.107
  38.6 2.5 while.107
  41.4 1.8 convolution_convert_fusion.1
  44.6 27.5 %while.106 = (s32[]{:T(128)}, f32[2,1,128]{2,1,0:T(1,128)S(1)}, f32[2,1,128,96]{2,0,3,1:T(2,128)}, s32[2]{0:T(128)}, s32[2]{0:T(128)}, /*index=5*/bf16[2,1,128,9...) while((s32[]{:T(128)}, f32[2,1,128]{2,1,0:T(1,128)S(1)}, ...), condition=%wide.region_14.15_spmd, body=%wide.region_10.14_spmd.sunk | while | flops 25573404 | bytes 785178 | solution.py:101
  50.2 4.8 %while.108 = (s32[]{:T(128)}, f32[1,128]{1,0:T(1,128)}, f32[1,128,96]{1,2,0:T(8,128)S(1)}, s32[]{:T(128)}, s32[]{:T(128)}, /*index=5*/s32[]{:T(128)}, bf16[2048,...) while((s32[]{:T(128)}, f32[1,128]{1,0:T(1,128)}, ...), condition=%wide.region_13.13_spmd, body=%wide.region_11.12_spmd.sunk | while | flops 25573384 | bytes 585471 | solution.py:90
  55.7 2.7 dynamic_update_slice.39
  63.9 4.8 %while.108 = (s32[]{:T(128)}, f32[1,128]{1,0:T(1,128)}, f32[1,128,96]{1,2,0:T(8,128)S(1)}, s32[]{:T(128)}, s32[]{:T(128)}, /*index=5*/s32[]{:T(128)}, bf16[2048,...) while((s32[]{:T(128)}, f32[1,128]{1,0:T(1,128)}, ...), condition=%wide.region_13.13_spmd, body=%wide.region_11.12_spmd.sunk | while | flops 25573384 | bytes 585471 | solution.py:90
  69.4 2.7 dynamic_update_slice.39
  75.9 2.2 fusion.106
  83.4 83.3 %all-reduce.3.cloned.1.call-done = f32[128,1536]{1,0:T(8,128)} async-done(((f32[128,1536]{1,0:T(8,128)}), f32[128,1536]{1,0:T(8,128)}) %all-reduce.3.cloned.1.call-update) | async-done | bytes 786448 | tf_op jit(solution)/shard_map/psum | solution.py:229
  166.7 1.4 multiply_reduce_fusion
  169.3 1.6 gather_fusion.2
  172.9 10.0 %all-to-all-start = ((bf16[32,4,1536]{2,1,0:T(4,128)(2,1)}), bf16[32,4,1536]{2,1,0:T(4,128)(2,1)}, u32[]{:S(2)}, u32[]{:S(2)}) async-start(bf16[32,4,1536]{2,1,0:T(4,128)(2,1)} %all_to_all.14), calls=%async_computation | async-start | bytes 786432 | tf_op jit(solution)/shard_map/all_to_all | solution.py:269
  183.1 15.1 %all-to-all-done = bf16[32,4,1536]{2,1,0:T(4,128)(2,1)} async-done(((bf16[32,4,1536]{2,1,0:T(4,128)(2,1)}), bf16[32,4,1536]{2,1,0:T(4,128)(2,1)}, u32[]{:S(2)}, u32[]{:S(2)}) %all-to-all-start) | async-done | bytes 393248 | tf_op jit(solution)/shard_map/all_to_all | solution.py:269
  199.2 1.5 gather_fusion
  200.7 2.7 fusion.38
  203.4 3.5 convolution_convert_fusion
  208.0 58.5 %all-reduce.5.cloned.1.call-done = bf16[96,1536]{1,0:T(8,128)(2,1)} async-done(((bf16[96,1536]{1,0:T(8,128)(2,1)}), bf16[96,1536]{1,0:T(8,128)(2,1)}) %all-reduce.5.cloned.1.call-update) | async-done | bytes 294928 | tf_op jit(solution)/shard_map/psum | solution.py:114
  266.5 3.0 gather_fusion.1
  271.8 10.0 %all-to-all-start.1 = ((bf16[32,4,1536]{2,1,0:T(4,128)(2,1)}), bf16[32,4,1536]{2,1,0:T(4,128)(2,1)}, u32[]{:S(2)}, u32[]{:S(2)}) async-start(bf16[32,4,1536]{2,1,0:T(4,128)(2,1)} %select_select_fusion.1), calls=%async_computation.1 | async-start | bytes 786432 | tf_op jit(solution)/shard_map/all_to_all | solution.py:285
  281.7 1.3 compare_and_fusion.1
  283.9 1.5 convolution_convert_fusion.2
  285.4 12.0 %all-to-all-done.1 = bf16[32,4,1536]{2,1,0:T(4,128)(2,1)} async-done(((bf16[32,4,1536]{2,1,0:T(4,128)(2,1)}), bf16[32,4,1536]{2,1,0:T(4,128)(2,1)}, u32[]{:S(2)}, u32[]{:S(2)}) %all-to-all-start.1) | async-done | bytes 393248 | tf_op jit(solution)/shard_map/all_to_all | solution.py:285
  298.5 1.6 gather_fusion.3
  300.2 1.6 select_convert_fusion
  303.5 46.6 %all-gather = bf16[32,2,1536]{2,1,0:T(2,128)(2,1)S(1)} all-gather(bf16[1,2,1536]{2,1,0:T(2,128)(2,1)S(1)} %fusion.76), channel_id=1, replica_groups=mesh['req'=32,'vocab'=8] {'req'}, dimensions={0}, use_global_device_ids=true | all-gather | bytes 202752 | tf_op jit(solution)/shard_map/all_gather | solution.py:329
  351.3 72.8 %pmax.7 = f32[64,1]{0,1:T(1,128)} all-reduce(f32[64,1]{0,1:T(1,128)S(1)} %bitcast.225), channel_id=1, replica_groups=mesh['req'=32,'vocab'=8] {'req'}, use_global_device_ids=true, to_apply=%region_32.34 | all-reduce | flops 64 | bytes 512 | tf_op jit(solution)/shard_map/pmax | solution.py:335
  (182 shorter events, 63.2 us)
Async XLA Ops:
  7.2 343.0 %copy-start = (bf16[1536,1000]{0,1:T(8,128)(2,1)S(1)}, bf16[1536,1000]{0,1:T(8,128)(2,1)}, u32[]{:S(2)}) copy-start(bf16[1536,1000]{0,1:T(8,128)(2,1)} %param.45) | copy-start | bytes 9216004
  7.2 13.1 %copy-start.1 = (bf16[2,64,1536]{2,1,0:T(8,128)(2,1)S(1)}, bf16[2,64,1536]{2,1,0:T(8,128)(2,1)}, u32[]{:S(2)}) copy-start(bf16[2,64,1536]{2,1,0:T(8,128)(2,1)} %param.28) | copy-start | bytes 1179652
  7.2 159.5 %all-reduce.3.cloned.1.call-start = ((), (), s32[]{:S(2)}) async-start(), calls=%async_computation.2 | async-start | bytes 1572864 | tf_op jit(solution)/shard_map/psum | solution.py:229
  11.6 2.9 copy-start.17
  12.9 10.4 %copy-start.14 = (f32[1536]{0:T(1024)}, f32[1536]{0:T(1024)S(1)}, u32[]{:S(2)}) copy-start(f32[1536]{0:T(1024)S(1)} %convert_element_type.141) | copy-start | bytes 18436
  24.8 2.3 copy-start.4
  27.1 14.0 %copy-start.15 = (f32[1536]{0:T(1024)S(1)}, f32[1536]{0:T(1024)}, u32[]{:S(2)}) copy-start(f32[1536]{0:T(1024)} %copy-done.14) | copy-start | bytes 18436
  27.1 14.0 %copy-start.23 = (f32[128]{0:T(128)S(1)}, f32[128]{0:T(128)}, u32[]{:S(2)}) copy-start(f32[128]{0:T(128)} %rsqrt.28) | copy-start | bytes 1540
  41.1 2.1 copy-start.8
  41.1 2.3 copy-start.20
  41.2 2.3 copy-start.21
  41.2 2.5 copy-start.5
  41.2 2.5 copy-start.6
  41.2 2.5 copy-start.7
  43.6 1.0 copy-start.9
  43.7 0.9 copy-start.11
  72.1 6.1 %copy-start.22 = (s32[64]{0:T(128)S(1)}, s32[64]{0:T(128)}, u32[]{:S(2)}) copy-start(s32[64]{0:T(128)} %param.30) | copy-start | bytes 772
  73.1 10.0 %copy-start.18 = (bf16[1536]{0:T(1024)(128)(2,1)S(1)}, bf16[1536]{0:T(1024)(128)(2,1)}, u32[]{:S(2)}) copy-start(bf16[1536]{0:T(1024)(128)(2,1)} %param.36) | copy-start | bytes 9220
  166.7 1.4 copy-start.2
  172.9 25.2 %all-to-all-start = ((bf16[32,4,1536]{2,1,0:T(4,128)(2,1)}), bf16[32,4,1536]{2,1,0:T(4,128)(2,1)}, u32[]{:S(2)}, u32[]{:S(2)}) async-start(bf16[32,4,1536]{2,1,0:T(4,128)(2,1)} %all_to_all.14), calls=%async_computation | async-start | bytes 786432 | tf_op jit(solution)/shard_map/all_to_all | solution.py:269
  182.9 83.6 %all-reduce.5.cloned.1.call-start = ((), (), s32[]{:S(2)}) async-start(), calls=%async_computation.3 | async-start | bytes 589824 | tf_op jit(solution)/shard_map/psum | solution.py:114
  200.7 2.7 copy-start.3
  203.4 3.6 copy-start.13
  203.4 4.3 %copy-start.12 = (bf16[128,1,48]{0,2,1:T(8,128)(2,1)S(1)}, bf16[128,1,48]{0,2,1:T(8,128)(2,1)}, u32[]{:S(2)}) copy-start(bf16[128,1,48]{0,2,1:T(8,128)(2,1)} %copy-done.11) | copy-start | bytes 36868
  203.4 4.4 %copy-start.10 = (bf16[128,1,48]{0,2,1:T(8,128)(2,1)S(1)}, bf16[128,1,48]{0,2,1:T(8,128)(2,1)}, u32[]{:S(2)}) copy-start(bf16[128,1,48]{0,2,1:T(8,128)(2,1)} %copy-done.9) | copy-start | bytes 36868
  203.4 4.6 %copy-start.19 = (bf16[1536]{0:T(1024)(128)(2,1)S(1)}, bf16[1536]{0:T(1024)(128)(2,1)}, u32[]{:S(2)}) copy-start(bf16[1536]{0:T(1024)(128)(2,1)} %param.37) | copy-start | bytes 9220
  269.5 13.6 %copy-start.16 = (s32[2,8]{1,0:T(2,128)S(1)}, s32[2,8]{1,0:T(2,128)}, u32[]{:S(2)}) copy-start(s32[2,8]{1,0:T(2,128)} %param.31) | copy-start | bytes 196
  271.8 25.7 %all-to-all-start.1 = ((bf16[32,4,1536]{2,1,0:T(4,128)(2,1)}), bf16[32,4,1536]{2,1,0:T(4,128)(2,1)}, u32[]{:S(2)}, u32[]{:S(2)}) async-start(bf16[32,4,1536]{2,1,0:T(4,128)(2,1)} %select_select_fusion.1), calls=%async_computation.1 | async-start | bytes 786432 | tf_op jit(solution)/shard_map/all_to_all | solution.py:285
Sparse Core Ops, SparseCore 0:
  78.3 88.3 all-reduce.2
  207.1 59.3 all-reduce.4
where the time goes:
time: 433 us; the launch traced here: 431 us
  waiting for transfers between devices  169 us (39%)
  blocking collectives  119 us (27%)
  local copies, waits for them, and re-layouts  44.3 us (10%)
  other arithmetic  26.9 us (6%)
  matrix products  26.9 us (6%)
  starting transfers between devices  20 us (5%)
  between operations  14.6 us (3%)
  loops' own time  9.85 us (2%)
    psum x1, waiting for transfers between devices, per_device(): residual = states + lax.psum(attend_part, 'vocab')  83.3 us
    pmax x1, blocking collectives, per_device(): lax.pmax(local_max, 'req')  72.8 us
    psum x1, waiting for transfers between devices, feed_forward(): summed = lax.psum(partial_sum.astype(jnp.bfloat16), 'vocab')  58.5 us
    all_gather x1, blocking collectives, per_device(): lax.all_gather(head_in, 'req', axis=0, tiled=True)  46.6 us
    all_to_all x1, waiting for transfers between devices, per_device(): lax.all_to_all(outgoing, 'req', split_axis=0, concat_axis=0, tiled=True)  15.1 us
    all_to_all x1, waiting for transfers between devices, per_device(): lax.all_to_all(backward, 'req', split_axis=0, concat_axis=0, tiled=True)  12 us
    dynamic_slice x8, local copies, waits for them, and re-layouts, maxima_over(): lax.map(lambda item: span_max(item[0], item[1], item[2], joined_keys, blo...  10 us
    all_to_all x1, starting transfers between devices, per_device(): lax.all_to_all(backward, 'req', split_axis=0, concat_axis=0, tiled=True)  9.96 us
  transfers between devices with their start and end apart: 4, of which 4 were waited for; matrix products, arithmetic and copies ran while one was open for 2% of the time, Pallas kernels for 0%

commit v1 on v0

--- a/solution.py
+++ b/solution.py
@@ -111,7 +111,8 @@
     up_out = jnp.dot(hidden_in, up_weight, preferred_element_type=jnp.float32)
     hidden = (jax.nn.silu(gate_out) * up_out).astype(jnp.bfloat16)
     partial_sum = jnp.dot(hidden, down_weight, preferred_element_type=jnp.float32)
-    summed = lax.psum(partial_sum.astype(jnp.bfloat16), "vocab")
+    slab_in = partial_sum.astype(jnp.bfloat16)
+    summed = lax.all_gather(slab_in, axis_name="vocab").sum(axis=0)
     return summed
 
 

time: 433 us -> 398 us (0.919)
  waiting for transfers between devices: 169 us -> 132 us
    psum x1 -> x0, waiting for transfers between devices: 58.5 us -> none  [feed_forward(): summed = lax.psum(partial_sum.astype(jnp.bfloat16), 'vocab')]
    all_gather x0 -> x1, waiting for transfers between devices: none -> 22.6 us  [feed_forward(): summed = lax.all_gather(slab_in, axis_name='vocab').sum(axis=0)]
where the time goes in v1:
time: 398 us; the launch traced here: 395 us
  waiting for transfers between devices  132 us (33%)
  blocking collectives  120 us (30%)
  local copies, waits for them, and re-layouts  42.9 us (11%)
  other arithmetic  28.9 us (7%)
  matrix products  26.9 us (7%)
  starting transfers between devices  20 us (5%)
  between operations  14.6 us (4%)
  loops' own time  9.85 us (2%)
    psum x1, waiting for transfers between devices, per_device(): residual = states + lax.psum(attend_part, 'vocab')  83.7 us
    pmax x1, blocking collectives, per_device(): lax.pmax(local_max, 'req')  72.8 us
    all_gather x1, blocking collectives, per_device(): lax.all_gather(head_in, 'req', axis=0, tiled=True)  47.1 us
    all_gather x1, waiting for transfers between devices, feed_forward(): summed = lax.all_gather(slab_in, axis_name='vocab').sum(axis=0)  22.6 us
    all_to_all x1, waiting for transfers between devices, per_device(): lax.all_to_all(outgoing, 'req', split_axis=0, concat_axis=0, tiled=True)  15 us
    all_to_all x1, waiting for transfers between devices, per_device(): lax.all_to_all(backward, 'req', split_axis=0, concat_axis=0, tiled=True)  10.7 us
    dynamic_slice x8, local copies, waits for them, and re-layouts, maxima_over(): lax.map(lambda item: span_max(item[0], item[1], item[2], joined_keys, blo...  10 us
    all_to_all x1, starting transfers between devices, per_device(): lax.all_to_all(backward, 'req', split_axis=0, concat_axis=0, tiled=True)  9.96 us
  transfers between devices with their start and end apart: 4, of which 4 were waited for; matrix products, arithmetic and copies ran while one was open for 2% of the time, Pallas kernels for 0%

profile of v1, /device:TPU:6, one launch (start us, length us, event | category | flops | bytes accessed | tf_op | source)
XLA Modules:
  0.0 395.2 jit_solution(8013796173126080211)
XLA Ops:
  7.8 1.4 reduce-window.24
  18.8 1.4 copy.72
  21.9 1.4 fusion.105
  25.5 1.6 maximum_bitcast_fusion
  27.1 14.0 %while.104 = (s32[]{:T(128)}, f32[2,1,128]{2,1,0:T(1,128)S(1)}, s32[2]{0:T(128)}, s32[2]{0:T(128)}, bf16[2,1,128,96]{3,2,1,0:T(8,128)(2,1)}, /*index=5*/bf16[204...) while((s32[]{:T(128)}, f32[2,1,128]{2,1,0:T(1,128)S(1)}, ...), condition=%wide.region_9.10_spmd, body=%wide.region_5.9_spmd.sunk | while | flops 12781597 | bytes 177346 | solution.py:94
  31.6 2.5 while.107
  38.6 2.5 while.107
  41.4 1.8 convolution_convert_fusion.1
  44.6 27.5 %while.106 = (s32[]{:T(128)}, f32[2,1,128]{2,1,0:T(1,128)S(1)}, f32[2,1,128,96]{2,0,3,1:T(2,128)}, s32[2]{0:T(128)}, s32[2]{0:T(128)}, /*index=5*/bf16[2,1,128,9...) while((s32[]{:T(128)}, f32[2,1,128]{2,1,0:T(1,128)S(1)}, ...), condition=%wide.region_14.15_spmd, body=%wide.region_10.14_spmd.sunk | while | flops 25573404 | bytes 785178 | solution.py:101
  50.2 4.8 %while.108 = (s32[]{:T(128)}, f32[1,128]{1,0:T(1,128)}, f32[1,128,96]{1,2,0:T(8,128)S(1)}, s32[]{:T(128)}, s32[]{:T(128)}, /*index=5*/s32[]{:T(128)}, bf16[2048,...) while((s32[]{:T(128)}, f32[1,128]{1,0:T(1,128)}, ...), condition=%wide.region_13.13_spmd, body=%wide.region_11.12_spmd.sunk | while | flops 25573384 | bytes 585471 | solution.py:90
  55.7 2.7 dynamic_update_slice.39
  63.9 4.8 %while.108 = (s32[]{:T(128)}, f32[1,128]{1,0:T(1,128)}, f32[1,128,96]{1,2,0:T(8,128)S(1)}, s32[]{:T(128)}, s32[]{:T(128)}, /*index=5*/s32[]{:T(128)}, bf16[2048,...) while((s32[]{:T(128)}, f32[1,128]{1,0:T(1,128)}, ...), condition=%wide.region_13.13_spmd, body=%wide.region_11.12_spmd.sunk | while | flops 25573384 | bytes 585471 | solution.py:90
  69.4 2.7 dynamic_update_slice.39
  75.9 2.2 fusion.106
  83.0 83.7 %all-reduce.2.cloned.1.call-done = f32[128,1536]{1,0:T(8,128)} async-done(((f32[128,1536]{1,0:T(8,128)}), f32[128,1536]{1,0:T(8,128)}) %all-reduce.2.cloned.1.call-update) | async-done | bytes 786448 | tf_op jit(solution)/shard_map/psum | solution.py:230
  166.7 1.4 multiply_reduce_fusion
  169.3 1.6 gather_fusion.2
  172.9 10.0 %all-to-all-start = ((bf16[32,4,1536]{2,1,0:T(4,128)(2,1)}), bf16[32,4,1536]{2,1,0:T(4,128)(2,1)}, u32[]{:S(2)}, u32[]{:S(2)}) async-start(bf16[32,4,1536]{2,1,0:T(4,128)(2,1)} %all_to_all.14), calls=%async_computation | async-start | bytes 786432 | tf_op jit(solution)/shard_map/all_to_all | solution.py:270
  183.1 15.0 %all-to-all-done = bf16[32,4,1536]{2,1,0:T(4,128)(2,1)} async-done(((bf16[32,4,1536]{2,1,0:T(4,128)(2,1)}), bf16[32,4,1536]{2,1,0:T(4,128)(2,1)}, u32[]{:S(2)}, u32[]{:S(2)}) %all-to-all-start) | async-done | bytes 393248 | tf_op jit(solution)/shard_map/all_to_all | solution.py:270
  199.1 1.5 gather_fusion
  200.7 2.6 fusion.38
  203.3 3.5 convolution_convert_fusion
  208.3 22.6 %all-gather.4.cloned.1.call-done = bf16[768,1536]{1,0:T(8,128)(2,1)} async-done(((bf16[96,1536]{1,0:T(8,128)(2,1)}), bf16[768,1536]{1,0:T(8,128)(2,1)}) %all-gather.4.cloned.1.call-update) | async-done | bytes 2359312 | tf_op jit(solution)/shard_map/all_gather | solution.py:115
  230.9 2.0 reduce_sum.182
  233.0 1.6 gather_fusion.1
  236.8 10.0 %all-to-all-start.1 = ((bf16[32,4,1536]{2,1,0:T(4,128)(2,1)}), bf16[32,4,1536]{2,1,0:T(4,128)(2,1)}, u32[]{:S(2)}, u32[]{:S(2)}) async-start(bf16[32,4,1536]{2,1,0:T(4,128)(2,1)} %select_select_fusion.1), calls=%async_computation.1 | async-start | bytes 786432 | tf_op jit(solution)/shard_map/all_to_all | solution.py:286
  249.0 1.5 convolution_convert_fusion.2
  250.5 10.7 %all-to-all-done.1 = bf16[32,4,1536]{2,1,0:T(4,128)(2,1)} async-done(((bf16[32,4,1536]{2,1,0:T(4,128)(2,1)}), bf16[32,4,1536]{2,1,0:T(4,128)(2,1)}, u32[]{:S(2)}, u32[]{:S(2)}) %all-to-all-start.1) | async-done | bytes 393248 | tf_op jit(solution)/shard_map/all_to_all | solution.py:286
  262.3 1.6 gather_fusion.3
  264.0 1.6 select_convert_fusion
  267.3 47.1 %all-gather.1 = bf16[32,2,1536]{2,1,0:T(2,128)(2,1)S(1)} all-gather(bf16[1,2,1536]{2,1,0:T(2,128)(2,1)S(1)} %fusion.76), channel_id=1, replica_groups=mesh['req'=32,'vocab'=8] {'req'}, dimensions={0}, use_global_device_ids=true | all-gather | bytes 202752 | tf_op jit(solution)/shard_map/all_gather | solution.py:330
  315.6 72.8 %pmax.7 = f32[64,1]{0,1:T(1,128)} all-reduce(f32[64,1]{0,1:T(1,128)S(1)} %bitcast.227), channel_id=1, replica_groups=mesh['req'=32,'vocab'=8] {'req'}, use_global_device_ids=true, to_apply=%region_32.34 | all-reduce | flops 64 | bytes 512 | tf_op jit(solution)/shard_map/pmax | solution.py:336
  (183 shorter events, 64.5 us)
Async XLA Ops:
  7.2 307.3 %copy-start = (bf16[1536,1000]{0,1:T(8,128)(2,1)S(1)}, bf16[1536,1000]{0,1:T(8,128)(2,1)}, u32[]{:S(2)}) copy-start(bf16[1536,1000]{0,1:T(8,128)(2,1)} %param.45) | copy-start | bytes 9216004
  7.2 13.1 %copy-start.1 = (bf16[2,64,1536]{2,1,0:T(8,128)(2,1)S(1)}, bf16[2,64,1536]{2,1,0:T(8,128)(2,1)}, u32[]{:S(2)}) copy-start(bf16[2,64,1536]{2,1,0:T(8,128)(2,1)} %param.28) | copy-start | bytes 1179652
  7.2 159.5 %all-reduce.2.cloned.1.call-start = ((), (), s32[]{:S(2)}) async-start(), calls=%async_computation.2 | async-start | bytes 1572864 | tf_op jit(solution)/shard_map/psum | solution.py:230
  11.6 2.9 copy-start.17
  12.9 10.4 %copy-start.14 = (f32[1536]{0:T(1024)}, f32[1536]{0:T(1024)S(1)}, u32[]{:S(2)}) copy-start(f32[1536]{0:T(1024)S(1)} %convert_element_type.143) | copy-start | bytes 18436
  24.8 2.3 copy-start.4
  27.1 14.0 %copy-start.15 = (f32[1536]{0:T(1024)S(1)}, f32[1536]{0:T(1024)}, u32[]{:S(2)}) copy-start(f32[1536]{0:T(1024)} %copy-done.14) | copy-start | bytes 18436
  27.1 14.0 %copy-start.23 = (f32[128]{0:T(128)S(1)}, f32[128]{0:T(128)}, u32[]{:S(2)}) copy-start(f32[128]{0:T(128)} %rsqrt.28) | copy-start | bytes 1540
  41.1 2.1 copy-start.8
  41.1 2.3 copy-start.20
  41.2 2.3 copy-start.21
  41.2 2.5 copy-start.5
  41.2 2.5 copy-start.6
  41.2 2.5 copy-start.7
  43.6 1.0 copy-start.9
  43.7 0.9 copy-start.11
  72.1 6.1 %copy-start.22 = (s32[64]{0:T(128)S(1)}, s32[64]{0:T(128)}, u32[]{:S(2)}) copy-start(s32[64]{0:T(128)} %param.30) | copy-start | bytes 772
  73.1 9.8 %copy-start.18 = (bf16[1536]{0:T(1024)(128)(2,1)S(1)}, bf16[1536]{0:T(1024)(128)(2,1)}, u32[]{:S(2)}) copy-start(bf16[1536]{0:T(1024)(128)(2,1)} %param.36) | copy-start | bytes 9220
  166.7 1.4 copy-start.2
  172.9 25.2 %all-to-all-start = ((bf16[32,4,1536]{2,1,0:T(4,128)(2,1)}), bf16[32,4,1536]{2,1,0:T(4,128)(2,1)}, u32[]{:S(2)}, u32[]{:S(2)}) async-start(bf16[32,4,1536]{2,1,0:T(4,128)(2,1)} %all_to_all.14), calls=%async_computation | async-start | bytes 786432 | tf_op jit(solution)/shard_map/all_to_all | solution.py:270
  182.8 48.1 %all-gather.4.cloned.1.call-start = ((), (), s32[]{:S(2)}) async-start(), calls=%async_computation.3 | async-start | bytes 2654208 | tf_op jit(solution)/shard_map/all_gather | solution.py:115
  200.7 2.6 copy-start.3
  203.3 3.6 copy-start.13
  203.3 4.3 %copy-start.12 = (bf16[128,1,48]{0,2,1:T(8,128)(2,1)S(1)}, bf16[128,1,48]{0,2,1:T(8,128)(2,1)}, u32[]{:S(2)}) copy-start(bf16[128,1,48]{0,2,1:T(8,128)(2,1)} %copy-done.11) | copy-start | bytes 36868
  203.3 4.4 %copy-start.10 = (bf16[128,1,48]{0,2,1:T(8,128)(2,1)S(1)}, bf16[128,1,48]{0,2,1:T(8,128)(2,1)}, u32[]{:S(2)}) copy-start(bf16[128,1,48]{0,2,1:T(8,128)(2,1)} %copy-done.9) | copy-start | bytes 36868
  203.3 4.5 %copy-start.19 = (bf16[1536]{0:T(1024)(128)(2,1)S(1)}, bf16[1536]{0:T(1024)(128)(2,1)}, u32[]{:S(2)}) copy-start(bf16[1536]{0:T(1024)(128)(2,1)} %param.37) | copy-start | bytes 9220
  234.6 13.6 %copy-start.16 = (s32[2,8]{1,0:T(2,128)S(1)}, s32[2,8]{1,0:T(2,128)}, u32[]{:S(2)}) copy-start(s32[2,8]{1,0:T(2,128)} %param.31) | copy-start | bytes 196
  236.8 24.4 %all-to-all-start.1 = ((bf16[32,4,1536]{2,1,0:T(4,128)(2,1)}), bf16[32,4,1536]{2,1,0:T(4,128)(2,1)}, u32[]{:S(2)}, u32[]{:S(2)}) async-start(bf16[32,4,1536]{2,1,0:T(4,128)(2,1)} %select_select_fusion.1), calls=%async_computation.1 | async-start | bytes 786432 | tf_op jit(solution)/shard_map/all_to_all | solution.py:286
Sparse Core Ops, SparseCore 0:
  78.3 88.3 all-reduce.1
  207.0 23.8 all-gather.3
